TPU v7x, 256 devices: a whole 4x4x8 slice. The times are simulated.
256 devices in a mesh: kv: 2 (over core), pg: 128 (over x, z, y).
Axes of the slice: x: 4, y: 4, z: 8, core: 2. Of those that a mesh axis runs over, the one named last changes fastest.
Arguments:
- layer_hidden_input: bfloat16 [16384, 2560], P('pg'), may hold values from -6 to 6
- norm_scale_vector: float32 [2560], replicated, may hold values from 0.1 to 1.9
- expert_choice_index: int32 [16384, 6], P('pg'), may hold values from 0 to 63, all different within a row; in each aligned block of 128 rows (0 to 127, 128 to 255, ...) at most 16 rows name the same one
- expert_choice_weight: float32 [16384, 6], P('pg'), may hold values from 0.05 to 0.35
- request_of_token: int32 [16384], P('pg'), may hold values from 0 to 255, never falling along the last dimension, each value on 1 to 512 neighbouring positions
- adapter_of_request: int32 [256], replicated, may hold values from 0 to 63
- adapter_of_slot: int32 [128], replicated, may hold values from 0 to 63, as said below
- expert_gate_up_weight: bfloat16 [128, 2560, 2, 768], P('pg', None, None, 'kv'), may hold values from -0.125 to 0.125
- expert_down_weight: bfloat16 [128, 768, 2560], P('pg', 'kv'), may hold values from -0.15625 to 0.15625
- adapter_down_weight: bfloat16 [128, 2560, 8], P('pg'), may hold values from -0.125 to 0.125
- adapter_up_weight: bfloat16 [128, 8, 2560], P('pg', None, 'kv'), may hold values from -0.75 to 0.75
Outputs:
- mixed: bfloat16 [16384, 2560], P('pg', 'kv')
Inputs may be any that keep to these rules, and one draw needn't show every extreme that they name: `expert_choice_index`: each row names 6 different experts. The 128 rows of one index of pg name one expert at most 16 times; some expert is named exactly 16 times by the rows of some index. `adapter_of_slot`: every adapter is held by exactly two slots. `request_of_token`: tokens of one request stand in a row; request numbers never fall along the tokens.
All inputs are finite; a program needn't handle non-finite values.
Results may differ from a plain program's by a relative error of at most 0.013.
Values may be sent and summed in bfloat16 or wider, within the bound.
No kernel may reach another device: no remote copies, remote signals or barrier semaphores. Data moves between devices by JAX's collectives and lax.ppermute only.
A program may use at most 128 MiB of HBM per device.

v0:
```python
import jax
import jax.numpy as jnp
from jax import lax
from jax.sharding import PartitionSpec as P

PG_AXES = ("px", "pz", "py")


def normalize(states, gain_vector):
    values = states.astype(jnp.float32)
    inverse_rms = lax.rsqrt(jnp.mean(values * values, axis=-1, keepdims=True) + 1e-06)
    return (values * inverse_rms * gain_vector).astype(jnp.bfloat16)


def expert_half(expert_rows, expert_gate_up_weight, expert_down_weight):
    gate_up = jnp.einsum(
        "rd,dgf->rgf", expert_rows, expert_gate_up_weight[0], preferred_element_type=jnp.float32
    )
    hidden = (jax.nn.silu(gate_up[:, 0]) * gate_up[:, 1]).astype(jnp.bfloat16)
    local_units = hidden.shape[1]
    piece_count = 2 // lax.axis_size("kv")
    piece_units = local_units // piece_count
    quarter = jnp.dot(
        hidden, expert_down_weight[0, 0:piece_units], preferred_element_type=jnp.float32
    )
    summed = quarter.astype(jnp.bfloat16).astype(jnp.float32)
    return lax.psum_scatter(summed.astype(jnp.bfloat16), "kv", scatter_dimension=1, tiled=True)


def rank_in_expert(flat_ids, expert_count):
    onehot = (flat_ids[:, None] == jnp.arange(expert_count, dtype=jnp.int32)[None, :]).astype(
        jnp.bfloat16
    )
    entries = flat_ids.shape[0]
    lower = (
        jnp.arange(entries, dtype=jnp.int32)[:, None]
        >= jnp.arange(entries, dtype=jnp.int32)[None, :]
    ).astype(jnp.bfloat16)
    running = jnp.dot(lower, onehot, preferred_element_type=jnp.float32)
    return (jnp.sum(running * onehot.astype(jnp.float32), axis=1) - 1.0).astype(jnp.int32)


def place_rows(slot_table, slot_total, normalized_input):
    slot_ids = jnp.arange(slot_total, dtype=jnp.int32)
    hits = jnp.zeros((slot_total, slot_table[0].shape[0]), jnp.float32)
    for table in slot_table:
        hits = hits + jnp.sum(
            (table[None, :, :] == slot_ids[:, None, None]).astype(jnp.float32), axis=2
        )
    placed = jnp.dot(
        hits.astype(jnp.bfloat16), normalized_input, preferred_element_type=jnp.float32
    )
    return placed.astype(jnp.bfloat16)


def collect_rows(slot_table, slot_total, weights, gathered):
    slot_ids = jnp.arange(slot_total, dtype=jnp.int32)
    combine = jnp.zeros((weights.shape[0], slot_total), jnp.float32)
    for table in slot_table:
        combine = combine + jnp.sum(
            jnp.where(table[:, :, None] == slot_ids[None, None, :], weights[:, :, None], 0.0),
            axis=1,
        )
    upper_part = combine.astype(jnp.bfloat16)
    lower_part = (combine - upper_part.astype(jnp.float32)).astype(jnp.bfloat16)
    return jnp.dot(upper_part, gathered, preferred_element_type=jnp.float32) + jnp.dot(
        lower_part, gathered, preferred_element_type=jnp.float32
    )


def on_device(
    layer_hidden_input,
    norm_scale_vector,
    expert_choice_index,
    expert_choice_weight,
    request_of_token,
    adapter_of_request,
    adapter_of_slot,
    expert_gate_up_weight,
    expert_down_weight,
    adapter_down_weight,
    adapter_up_weight,
):
    tok_rows, model_width = layer_hidden_input.shape
    top_count = expert_choice_index.shape[1]
    pg_size = lax.axis_size(PG_AXES)
    expert_count = pg_size // 2
    slot_cap = 4 * tok_rows * top_count // (3 * expert_count)
    half_width = model_width // lax.axis_size("kv")
    kv_index = lax.axis_index("kv")
    normalized_input = normalize(layer_hidden_input, norm_scale_vector)
    own_features = lax.dynamic_slice_in_dim(
        normalized_input, kv_index * half_width, half_width, axis=1
    )
    down_own = lax.dynamic_slice_in_dim(
        adapter_down_weight[0], kv_index * half_width, half_width, axis=0
    )
    rank_half = down_own.shape[1]
    packed = jnp.concatenate([down_own.T, adapter_up_weight[0]], axis=0)
    flat_ids = expert_choice_index.reshape(-1)
    slot_rank = rank_in_expert(flat_ids, expert_count)
    rank_table = slot_rank.reshape(tok_rows, top_count)
    first_slot = 2 * expert_choice_index * slot_cap + rank_table
    second_slot = first_slot + slot_cap
    slot_total = pg_size * slot_cap
    outbox = place_rows((first_slot, second_slot), slot_total, own_features).reshape(
        pg_size, slot_cap, half_width
    )
    inbox_half = lax.all_to_all(outbox, PG_AXES, split_axis=0, concat_axis=0, tiled=True)
    inbox_half, packed = lax.optimization_barrier((inbox_half, packed))
    packed_all = packed
    for axis_name in reversed(PG_AXES):
        packed_all = lax.all_gather(packed_all, axis_name, axis=0, tiled=False)
    packed_all = packed_all.reshape((pg_size,) + packed.shape)
    inbox_rows = lax.all_gather(
        inbox_half.reshape(pg_size * slot_cap, half_width), "kv", axis=1, tiled=True
    )
    half_out = expert_half(inbox_rows, expert_gate_up_weight, expert_down_weight)
    half_out, packed_all = lax.optimization_barrier((half_out, packed_all))
    results = lax.all_to_all(
        half_out.reshape(pg_size, slot_cap, half_width),
        PG_AXES,
        split_axis=0,
        concat_axis=0,
        tiled=True,
    )
    moe_sum = collect_rows(
        (first_slot, second_slot),
        slot_total,
        expert_choice_weight,
        results.reshape(slot_total, half_width),
    )
    request_count = adapter_of_request.shape[0]
    owner_table = request_of_token[:, None] == jnp.arange(request_count, dtype=jnp.int32)[None, :]
    token_adapter = jnp.sum(jnp.where(owner_table, adapter_of_request[None, :], 0), axis=1)
    slot_count = packed_all.shape[0]
    down_all = packed_all[:, 0:rank_half, :].reshape(slot_count * rank_half, half_width)
    up_all = packed_all[:, rank_half:, :].reshape(slot_count * rank_half, half_width)
    partial_rank = lax.dot_general(
        own_features, down_all, (((1,), (1,)), ((), ())), preferred_element_type=jnp.float32
    )
    rank_projected = lax.psum(partial_rank, "kv").reshape(tok_rows, slot_count, rank_half)
    matched = adapter_of_slot[None, :, None] == token_adapter[:, None, None]
    rank_projected = jnp.where(matched, rank_projected, 0.0).astype(jnp.bfloat16)
    flat_low = rank_projected.reshape(tok_rows, slot_count * rank_half)
    adapter_total_output = jnp.dot(flat_low, up_all, preferred_element_type=jnp.float32)
    return (moe_sum + adapter_total_output).astype(jnp.bfloat16)


def solution(mesh):
    kv_count = mesh.shape["kv"]
    pg_count = mesh.shape["pg"]
    y_count = 4 if pg_count % 4 == 0 else 1
    rest = pg_count // y_count
    z_count = 8 if rest % 8 == 0 else rest
    x_count = rest // z_count
    split_mesh = jax.sharding.Mesh(
        mesh.devices.reshape(kv_count, x_count, z_count, y_count), ("kv",) + PG_AXES
    )
    pg = PG_AXES
    placed = (
        P(pg, None),
        P(),
        P(pg, None),
        P(pg, None),
        P(pg),
        P(),
        P(),
        P(pg, None, None, "kv"),
        P(pg, "kv", None),
        P(pg, None, None),
        P(pg, None, "kv"),
    )
    return jax.shard_map(
        on_device, mesh=split_mesh, in_specs=placed, out_specs=P(pg, "kv"), check_vma=False
    )
```

profile of v0, /device:TPU:2, one launch (start us, length us, event | category | flops | bytes accessed | tf_op | source)
XLA Modules:
  0.0 468.3 jit_solution(15037000671731903780)
XLA Ops:
  6.5 1.4 convert_element_type.66
  7.9 1.8 multiply_reduce_fusion
  9.7 0.8 copy.50
  10.5 0.1 eq.98
  10.6 0.4 fusion.22
  11.0 0.1 convert_element_type.61
  11.1 0.1 copy.51
  11.2 0.7 broadcast_add_fusion
  11.9 0.8 dynamic-slice.1
  12.7 1.7 convert_reduce_fusion
  14.4 3.9 convolution_convert_fusion.1
  18.3 16.1 %all-to-all-start = ((bf16[128,16,1280]{2,1,0:T(8,128)(2,1)}), bf16[128,16,1280]{2,1,0:T(8,128)(2,1)}, u32[]{:S(2)}, u32[]{:S(2)}) async-start(bf16[128,16,1280]{2,1,0:T(8,128)(2,1)} %bitcast.33), calls=%async_computation | async-start | bytes 10485760 | tf_op jit(solution)/shard_map/all_to_all | solution.py:109
  34.5 119.2 %all-to-all-done = bf16[128,16,1280]{2,1,0:T(8,128)(2,1)} async-done(((bf16[128,16,1280]{2,1,0:T(8,128)(2,1)}), bf16[128,16,1280]{2,1,0:T(8,128)(2,1)}, u32[]{:S(2)}, u32[]{:S(2)}) %all-to-all-start) | async-done | bytes 5242912 | tf_op jit(solution)/shard_map/all_to_all | solution.py:109
  153.7 13.0 %all-gather = bf16[64,1280]{1,0:T(8,128)(2,1)} all-gather(bf16[16,1280]{1,0:T(8,128)(2,1)S(1)} %pad_maximum_fusion), channel_id=2, replica_groups=mesh['kv'=2,'px'=4,'pz'=8,'py'=4] {'py'}, dimensions={0}, use_global_device_ids=true | all-gather | bytes 204800 | tf_op jit(solution)/shard_map/all_gather | solution.py:113
  166.6 0.0 all-gather.7.cloned.1.call-start
  166.7 0.7 all-gather.7.cloned.1.call-update
  167.4 33.2 %all-gather.9.cloned.1.call-done = bf16[32,16,1280]{2,1,0:T(8,128)(2,1)} async-done(((bf16[4,16,1280]{2,1,0:T(8,128)(2,1)}), bf16[32,16,1280]{2,1,0:T(8,128)(2,1)}) %all-gather.9.cloned.1.call-update) | async-done | bytes 1310736 | tf_op jit(solution)/shard_map/all_gather | solution.py:113
  200.7 28.5 %all-gather.7.cloned.1.call-done = bf16[2048,2560]{1,0:T(8,128)(2,1)} async-done(((bf16[2048,1280]{1,0:T(8,128)(2,1)}), bf16[2048,2560]{1,0:T(8,128)(2,1)}) %all-gather.7.cloned.1.call-update) | async-done | bytes 10485776 | tf_op jit(solution)/shard_map/all_gather | solution.py:115
  229.1 12.2 %fusion = f32[2048,2,384]{2,0,1:T(8,128)S(1)} fusion(bf16[2048,2560]{1,0:T(8,128)(2,1)} %all-gather.7.cloned.1.call-done, bf16[2560,2,384]{2,1,0:T(2,128)(2,1)} %bitcast.40), kind=kOutput, calls=%fused_computation.1 | convolution fusion | flops 8053063680 | bytes 20709376 | tf_op jit(solution)/shard_map/rd,dgf->rgf/dot_general | solution.py:16
  241.3 8.2 %convolution_convert_fusion = bf16[2048,2560]{1,0:T(8,128)(2,1)} fusion(bf16[1,384,2560]{2,1,0:T(8,128)(2,1)S(1)} %copy-done, f32[2048,2,384]{2,0,1:T(8,128)S(1)} %fusion), kind=kOutput, calls=%fused_computation | convolution fusion | flops 4036493312 | bytes 18743296 | tf_op jit(solution)/shard_map/dot_general | solution.py:23
  249.5 41.8 %all-gather.11.cloned.1.call-done = bf16[32,4,16,1280]{3,2,1,0:T(8,128)(2,1)} async-done(((bf16[8,4,16,1280]{3,2,1,0:T(8,128)(2,1)}), bf16[32,4,16,1280]{3,2,1,0:T(8,128)(2,1)}) %all-gather.11.cloned.1.call-update) | async-done | bytes 5242896 | tf_op jit(solution)/shard_map/all_gather | solution.py:113
  291.3 27.9 %reduce-scatter.2.cloned.1.call-done = bf16[2048,1280]{1,0:T(8,128)(2,1)} async-done(((bf16[2048,2560]{1,0:T(8,128)(2,1)}), bf16[2048,1280]{1,0:T(8,128)(2,1)}) %reduce-scatter.2.cloned.1.call-update) | async-done | bytes 5242896 | tf_op jit(solution)/shard_map/reduce_scatter | solution.py:27
  319.2 14.4 %all-to-all-start.1 = ((bf16[128,16,1280]{2,1,0:T(8,128)(2,1)}), bf16[128,16,1280]{2,1,0:T(8,128)(2,1)}, u32[]{:S(2)}, u32[]{:S(2)}) async-start(bf16[128,16,1280]{2,1,0:T(8,128)(2,1)} %bitcast.34), calls=%async_computation.2 | async-start | bytes 10485760 | tf_op jit(solution)/shard_map/all_to_all | solution.py:120
  333.7 0.2 select_reduce_fusion.2
  333.9 0.7 broadcast_compare_fusion
  334.6 3.5 select_reduce_fusion
  338.0 2.9 fusion.18
  340.9 5.3 %all-reduce.1 = bf16[128,128,8]{0,2,1:T(8,128)(2,1)} all-reduce(f32[128,128,8]{0,2,1:T(8,128)S(1)} %fusion.18), channel_id=1, replica_groups=mesh['kv'=2,'px'=4,'pz'=8,'py'=4] {'kv'}, use_global_device_ids=true, to_apply=%region_8.9 | all-reduce | flops 131072 | bytes 786432 | tf_op jit(solution)/shard_map/psum | solution.py:142
  346.2 3.3 fusion.10
  349.5 104.3 %all-to-all-done.1 = bf16[128,16,1280]{2,1,0:T(8,128)(2,1)} async-done(((bf16[128,16,1280]{2,1,0:T(8,128)(2,1)}), bf16[128,16,1280]{2,1,0:T(8,128)(2,1)}, u32[]{:S(2)}, u32[]{:S(2)}) %all-to-all-start.1) | async-done | bytes 5242912 | tf_op jit(solution)/shard_map/all_to_all | solution.py:120
  453.8 3.8 fusion.26
  457.6 4.2 fusion.13
  (30 shorter events, 0.2 us)
Async XLA Ops:
  6.5 234.8 %copy-start = (bf16[1,384,2560]{2,1,0:T(8,128)(2,1)S(1)}, bf16[1,384,2560]{2,1,0:T(8,128)(2,1)}, u32[]{:S(2)}) copy-start(bf16[1,384,2560]{2,1,0:T(8,128)(2,1)} %param.19) | copy-start | bytes 5898244
  7.9 10.4 %copy-start.2 = (f32[128,2560]{1,0:T(8,128)}, f32[128,2560]{1,0:T(8,128)S(1)}, u32[]{:S(2)}) copy-start(f32[128,2560]{1,0:T(8,128)S(1)} %convert_element_type.66) | copy-start | bytes 3932164
  18.3 16.1 %copy-start.5 = (bf16[1,2560,8]{1,2,0:T(8,128)(2,1)S(1)}, bf16[1,2560,8]{1,2,0:T(8,128)(2,1)}, u32[]{:S(2)}) copy-start(bf16[1,2560,8]{1,2,0:T(8,128)(2,1)} %param.20) | copy-start | bytes 122884
  18.3 16.2 %copy-start.4 = (bf16[1,8,1280]{2,1,0:T(8,128)(2,1)S(1)}, bf16[1,8,1280]{2,1,0:T(8,128)(2,1)}, u32[]{:S(2)}) copy-start(bf16[1,8,1280]{2,1,0:T(8,128)(2,1)} %param.21) | copy-start | bytes 61444
  18.3 135.3 %all-to-all-start = ((bf16[128,16,1280]{2,1,0:T(8,128)(2,1)}), bf16[128,16,1280]{2,1,0:T(8,128)(2,1)}, u32[]{:S(2)}, u32[]{:S(2)}) async-start(bf16[128,16,1280]{2,1,0:T(8,128)(2,1)} %bitcast.33), calls=%async_computation | async-start | bytes 10485760 | tf_op jit(solution)/shard_map/all_to_all | solution.py:109
  34.4 166.2 %all-gather.9.cloned.1.call-start = ((), (), s32[]{:S(2)}) async-start(), calls=%async_computation.5 | async-start | bytes 1474560 | tf_op jit(solution)/shard_map/all_gather | solution.py:113
  166.6 62.5 %all-gather.7.cloned.1.call-start = ((), (), s32[]{:S(2)}) async-start(), calls=%async_computation.3 | async-start | bytes 15728640 | tf_op jit(solution)/shard_map/all_gather | solution.py:115
  167.4 123.9 %all-gather.11.cloned.1.call-start = ((), (), s32[]{:S(2)}) async-start(), calls=%async_computation.6 | async-start | bytes 6553600 | tf_op jit(solution)/shard_map/all_gather | solution.py:113
  200.6 118.6 %reduce-scatter.2.cloned.1.call-start = ((), (), s32[]{:S(2)}) async-start(), calls=%async_computation.4 | async-start | bytes 15728640 | tf_op jit(solution)/shard_map/reduce_scatter | solution.py:27
  319.2 14.4 %copy-start.7 = (s32[256]{0:T(256)S(1)}, s32[256]{0:T(256)}, u32[]{:S(2)}) copy-start(s32[256]{0:T(256)} %param.16) | copy-start | bytes 3076
  319.2 14.5 %copy-start.9 = (s32[128]{0:T(128)S(1)}, s32[128]{0:T(128)}, u32[]{:S(2)}) copy-start(s32[128]{0:T(128)} %param.15) | copy-start | bytes 1540
  319.2 14.6 %copy-start.8 = (s32[128]{0:T(128)S(1)}, s32[128]{0:T(128)}, u32[]{:S(2)}) copy-start(s32[128]{0:T(128)} %param.17) | copy-start | bytes 1540
  319.2 15.3 %copy-start.6 = (f32[128,6]{0,1:T(8,128)S(1)}, f32[128,6]{0,1:T(8,128)}, u32[]{:S(2)}) copy-start(f32[128,6]{0,1:T(8,128)} %param.14) | copy-start | bytes 9220
  319.2 134.5 %all-to-all-start.1 = ((bf16[128,16,1280]{2,1,0:T(8,128)(2,1)}), bf16[128,16,1280]{2,1,0:T(8,128)(2,1)}, u32[]{:S(2)}, u32[]{:S(2)}) async-start(bf16[128,16,1280]{2,1,0:T(8,128)(2,1)} %bitcast.34), calls=%async_computation.2 | async-start | bytes 10485760 | tf_op jit(solution)/shard_map/all_to_all | solution.py:120
  453.8 3.8 copy-start.1
  453.8 3.8 copy-start.3
Sparse Core Ops, SparseCore 0:
  166.8 33.7 all-gather.8
  202.4 26.7 all-gather.6
  231.0 60.3 all-gather.10
  293.7 25.4 reduce-scatter.1
where the time goes:
time: 469 us; the launch traced here: 468 us
  waiting for transfers between devices  356 us (76%)
  matrix products  38.7 us (8%)
  starting transfers between devices  30.6 us (7%)
  blocking collectives  18.3 us (4%)
  between operations  13.3 us (3%)
  other arithmetic  9.88 us (2%)
    all_to_all x1, waiting for transfers between devices, on_device(): lax.all_to_all(outbox, PG_AXES, split_axis=0, concat_axis=0, tiled=True)  119 us
    all_to_all x1, waiting for transfers between devices, on_device(): lax.all_to_all(half_out.reshape(pg_size, slot_cap, half_width), PG_AXES,...  104 us
    all_gather x2, waiting for transfers between devices, on_device(): packed_all = lax.all_gather(packed_all, axis_name, axis=0, tiled=False)  75 us
    all_gather x1, waiting for transfers between devices, on_device(): lax.all_gather(inbox_half.reshape(pg_size * slot_cap, half_width), 'kv',...  28.5 us
    reduce_scatter x1, waiting for transfers between devices, expert_half(): lax.psum_scatter(summed.astype(jnp.bfloat16), 'kv', scatter_dimension=1,...  27.9 us
    all_to_all x1, starting transfers between devices, on_device(): lax.all_to_all(outbox, PG_AXES, split_axis=0, concat_axis=0, tiled=True)  16.1 us
    all_to_all x1, starting transfers between devices, on_device(): lax.all_to_all(half_out.reshape(pg_size, slot_cap, half_width), PG_AXES,...  14.4 us
    all_gather x1, blocking collectives, on_device(): packed_all = lax.all_gather(packed_all, axis_name, axis=0, tiled=False)  13 us
  transfers between devices with their start and end apart: 6, of which 6 were waited for; matrix products, arithmetic and copies ran while one was open for 7% of the time, Pallas kernels for 0%

commit v1 on v0

--- a/solution.py
+++ b/solution.py
@@ -112,8 +112,14 @@
     for axis_name in reversed(PG_AXES):
         packed_all = lax.all_gather(packed_all, axis_name, axis=0, tiled=False)
     packed_all = packed_all.reshape((pg_size,) + packed.shape)
-    inbox_rows = lax.all_gather(
-        inbox_half.reshape(pg_size * slot_cap, half_width), "kv", axis=1, tiled=True
+    inbox_rows = jnp.concatenate(
+        lax.all_to_all(
+            jnp.stack([inbox_half.reshape(pg_size * slot_cap, half_width)] * lax.axis_size("kv")),
+            "kv",
+            0,
+            0,
+        ),
+        axis=1,
     )
     half_out = expert_half(inbox_rows, expert_gate_up_weight, expert_down_weight)
     half_out, packed_all = lax.optimization_barrier((half_out, packed_all))

time: 469 us -> 517 us (1.10)
  local copies, waits for them, and re-layouts: 1.95 us -> 99.2 us
  waiting for transfers between devices: 356 us -> 280 us
  blocking collectives: 18.3 us -> 32.8 us
  other arithmetic: 9.88 us -> 19 us
    reshape x0 -> x2, local copies, waits for them, and re-layouts: none -> 97.2 us  [on_device(): jnp.concatenate(lax.all_to_all(jnp.stack([inbox_half.reshape(pg_size * sl...]
    all_gather x2, waiting for transfers between devices: 75 us -> 33.9 us  [on_device(): packed_all = lax.all_gather(packed_all, axis_name, axis=0, tiled=False)]
    all_gather x1 -> x0, waiting for transfers between devices: 28.5 us -> none  [on_device(): lax.all_gather(inbox_half.reshape(pg_size * slot_cap, half_width), 'kv',...]
    all_to_all x0 -> x1, blocking collectives: none -> 14.5 us  [on_device(): lax.all_to_all(jnp.stack([inbox_half.reshape(pg_size * slot_cap, half_wid...]
    another operation x0 -> x1, other arithmetic: none -> 9.07 us  [on_device(): jnp.stack([inbox_half.reshape(pg_size * slot_cap, half_width)] * lax.axis...]
    reduce_scatter x1, waiting for transfers between devices: 27.9 us -> 22.7 us  [expert_half(): lax.psum_scatter(summed.astype(jnp.bfloat16), 'kv', scatter_dimension=1,...]
  transfers between devices with their start and end apart: 6 -> 5, of which waited for: 6 -> 4; matrix products, arithmetic and copies ran while one was open for 7% -> 27% of each run, Pallas kernels for 0% -> 0%
where the time goes in v1:
time: 517 us; the launch traced here: 516 us
  waiting for transfers between devices  280 us (54%)
  local copies, waits for them, and re-layouts  99.2 us (19%)
  matrix products  38.8 us (8%)
  blocking collectives  32.8 us (6%)
  starting transfers between devices  30.6 us (6%)
  other arithmetic  19 us (4%)
  between operations  15 us (3%)
    all_to_all x1, waiting for transfers between devices, on_device(): lax.all_to_all(outbox, PG_AXES, split_axis=0, concat_axis=0, tiled=True)  119 us
    all_to_all x1, waiting for transfers between devices, on_device(): lax.all_to_all(half_out.reshape(pg_size, slot_cap, half_width), PG_AXES,...  104 us
    reshape x2, local copies, waits for them, and re-layouts, on_device(): jnp.concatenate(lax.all_to_all(jnp.stack([inbox_half.reshape(pg_size * sl...  97.2 us
    all_gather x2, waiting for transfers between devices, on_device(): packed_all = lax.all_gather(packed_all, axis_name, axis=0, tiled=False)  33.9 us
    reduce_scatter x1, waiting for transfers between devices, expert_half(): lax.psum_scatter(summed.astype(jnp.bfloat16), 'kv', scatter_dimension=1,...  22.7 us
    all_to_all x1, starting transfers between devices, on_device(): lax.all_to_all(outbox, PG_AXES, split_axis=0, concat_axis=0, tiled=True)  16.1 us
    all_to_all x1, blocking collectives, on_device(): lax.all_to_all(jnp.stack([inbox_half.reshape(pg_size * slot_cap, half_wid...  14.5 us
    all_to_all x1, starting transfers between devices, on_device(): lax.all_to_all(half_out.reshape(pg_size, slot_cap, half_width), PG_AXES,...  14.4 us
  transfers between devices with their start and end apart: 5, of which 4 were waited for; matrix products, arithmetic and copies ran while one was open for 27% of the time, Pallas kernels for 0%

profile of v1, /device:TPU:2, one launch (start us, length us, event | category | flops | bytes accessed | tf_op | source)
XLA Modules:
  0.0 515.6 jit_solution(15852066076589916879)
XLA Ops:
  7.4 1.4 convert_element_type.66
  8.7 1.8 multiply_reduce_fusion
  10.5 0.8 copy.57
  11.3 0.1 eq.98
  11.4 0.4 fusion.21
  11.8 0.1 convert_element_type.61
  12.0 0.1 copy.58
  12.0 0.7 broadcast_add_fusion
  12.8 0.8 dynamic-slice.1
  13.5 1.7 convert_reduce_fusion
  15.2 3.9 convolution_convert_fusion.1
  19.2 16.1 %all-to-all-start = ((bf16[128,16,1280]{2,1,0:T(8,128)(2,1)}), bf16[128,16,1280]{2,1,0:T(8,128)(2,1)}, u32[]{:S(2)}, u32[]{:S(2)}) async-start(bf16[128,16,1280]{2,1,0:T(8,128)(2,1)} %bitcast.32), calls=%async_computation | async-start | bytes 10485760 | tf_op jit(solution)/shard_map/all_to_all | solution.py:109
  35.3 119.2 %all-to-all-done = bf16[128,16,1280]{2,1,0:T(8,128)(2,1)} async-done(((bf16[128,16,1280]{2,1,0:T(8,128)(2,1)}), bf16[128,16,1280]{2,1,0:T(8,128)(2,1)}, u32[]{:S(2)}, u32[]{:S(2)}) %all-to-all-start) | async-done | bytes 5242912 | tf_op jit(solution)/shard_map/all_to_all | solution.py:109
  154.5 13.0 %all-gather = bf16[64,1280]{1,0:T(8,128)(2,1)} all-gather(bf16[16,1280]{1,0:T(8,128)(2,1)S(1)} %pad_maximum_fusion.1), channel_id=2, replica_groups=mesh['kv'=2,'px'=4,'pz'=8,'py'=4] {'py'}, dimensions={0}, use_global_device_ids=true | all-gather | bytes 204800 | tf_op jit(solution)/shard_map/all_gather | solution.py:113
  167.5 33.9 %all-gather.6.cloned.1.call-done = bf16[32,16,1280]{2,1,0:T(8,128)(2,1)} async-done(((bf16[4,16,1280]{2,1,0:T(8,128)(2,1)}), bf16[32,16,1280]{2,1,0:T(8,128)(2,1)}) %all-gather.6.cloned.1.call-update) | async-done | bytes 1310736 | tf_op jit(solution)/shard_map/all_gather | solution.py:113
  201.5 9.1 %pad_maximum_fusion = bf16[2,2048,1280]{2,1,0:T(8,128)(2,1)} fusion(bf16[1,2048,1280]{2,1,0:T(8,128)(2,1)} %bitcast.4), kind=kLoop, calls=%fused_computation.1 | loop fusion | flops 5242880 | bytes 15728640 | tf_op jit(solution)/shard_map/stack | solution.py:117
  210.6 14.5 %all_to_all.15 = bf16[2,2048,1280]{2,1,0:T(8,128)(2,1)S(1)} all-to-all(bf16[2,2048,1280]{2,1,0:T(8,128)(2,1)} %pad_maximum_fusion), channel_id=1, replica_groups=mesh['kv'=2,'px'=4,'pz'=8,'py'=4] {'kv'}, dimensions={0} | all-to-all | bytes 20971520 | tf_op jit(solution)/shard_map/all_to_all | solution.py:116
  225.1 74.0 %copy.59 = bf16[2048,2,1280]{2,1,0:T(2,128)(2,1)} copy(bf16[2048,2,1280]{2,0,1:T(8,128)(2,1)S(1)} %bitcast.33) | data formatting | bytes 20971520 | tf_op jit(solution)/shard_map/reshape | solution.py:115
  299.0 23.2 %reshape.94 = bf16[2048,2560,1]{1,0,2:T(8,128)(2,1)} reshape(bf16[2048,2,1280]{2,1,0:T(2,128)(2,1)} %copy.59) | data formatting | bytes 20971520 | tf_op jit(solution)/shard_map/reshape | solution.py:115
  322.3 12.2 %fusion = f32[2048,2,384]{2,0,1:T(8,128)S(1)} fusion(bf16[2048,2560,1]{1,0,2:T(8,128)(2,1)} %reshape.94, bf16[2560,2,384]{2,1,0:T(2,128)(2,1)} %bitcast.40), kind=kOutput, calls=%fused_computation.11 | convolution fusion | flops 8053063680 | bytes 20709376 | tf_op jit(solution)/shard_map/rd,dgf->rgf/dot_general | solution.py:16
  334.4 8.2 %convolution_convert_fusion = bf16[2048,2560]{1,0:T(8,128)(2,1)} fusion(bf16[1,384,2560]{2,1,0:T(8,128)(2,1)S(1)} %copy-done, f32[2048,2,384]{2,0,1:T(8,128)S(1)} %fusion), kind=kOutput, calls=%fused_computation | convolution fusion | flops 4036493312 | bytes 18743296 | tf_op jit(solution)/shard_map/dot_general | solution.py:23
  342.7 22.7 %reduce-scatter.2.cloned.1.call-done = bf16[2048,1280]{1,0:T(8,128)(2,1)} async-done(((bf16[2048,2560]{1,0:T(8,128)(2,1)}), bf16[2048,1280]{1,0:T(8,128)(2,1)}) %reduce-scatter.2.cloned.1.call-update) | async-done | bytes 5242896 | tf_op jit(solution)/shard_map/reduce_scatter | solution.py:27
  365.4 14.4 %all-to-all-start.2 = ((bf16[128,16,1280]{2,1,0:T(8,128)(2,1)}), bf16[128,16,1280]{2,1,0:T(8,128)(2,1)}, u32[]{:S(2)}, u32[]{:S(2)}) async-start(bf16[128,16,1280]{2,1,0:T(8,128)(2,1)} %bitcast.34), calls=%async_computation.3 | async-start | bytes 10485760 | tf_op jit(solution)/shard_map/all_to_all | solution.py:126
  379.8 0.2 select_reduce_fusion.2
  380.0 0.7 broadcast_compare_fusion
  380.7 3.5 select_reduce_fusion
  384.2 2.9 fusion.17
  387.0 5.3 %all-reduce.1 = bf16[128,128,8]{0,2,1:T(8,128)(2,1)} all-reduce(f32[128,128,8]{0,2,1:T(8,128)S(1)} %fusion.17), channel_id=1, replica_groups=mesh['kv'=2,'px'=4,'pz'=8,'py'=4] {'kv'}, use_global_device_ids=true, to_apply=%region_8.9 | all-reduce | flops 131072 | bytes 786432 | tf_op jit(solution)/shard_map/psum | solution.py:148
  392.3 3.3 fusion.9
  395.6 104.5 %all-to-all-done.2 = bf16[128,16,1280]{2,1,0:T(8,128)(2,1)} async-done(((bf16[128,16,1280]{2,1,0:T(8,128)(2,1)}), bf16[128,16,1280]{2,1,0:T(8,128)(2,1)}, u32[]{:S(2)}, u32[]{:S(2)}) %all-to-all-start.2) | async-done | bytes 5242912 | tf_op jit(solution)/shard_map/all_to_all | solution.py:126
  500.1 3.8 fusion.25
  503.9 4.2 fusion.12
  (31 shorter events, 0.3 us)
Async XLA Ops:
  7.4 327.1 %copy-start = (bf16[1,384,2560]{2,1,0:T(8,128)(2,1)S(1)}, bf16[1,384,2560]{2,1,0:T(8,128)(2,1)}, u32[]{:S(2)}) copy-start(bf16[1,384,2560]{2,1,0:T(8,128)(2,1)} %param.19) | copy-start | bytes 5898244
  8.7 10.4 %copy-start.2 = (f32[128,2560]{1,0:T(8,128)}, f32[128,2560]{1,0:T(8,128)S(1)}, u32[]{:S(2)}) copy-start(f32[128,2560]{1,0:T(8,128)S(1)} %convert_element_type.66) | copy-start | bytes 3932164
  19.2 16.1 %copy-start.5 = (bf16[1,2560,8]{1,2,0:T(8,128)(2,1)S(1)}, bf16[1,2560,8]{1,2,0:T(8,128)(2,1)}, u32[]{:S(2)}) copy-start(bf16[1,2560,8]{1,2,0:T(8,128)(2,1)} %param.20) | copy-start | bytes 122884
  19.2 16.2 %copy-start.4 = (bf16[1,8,1280]{2,1,0:T(8,128)(2,1)S(1)}, bf16[1,8,1280]{2,1,0:T(8,128)(2,1)}, u32[]{:S(2)}) copy-start(bf16[1,8,1280]{2,1,0:T(8,128)(2,1)} %param.21) | copy-start | bytes 61444
  19.2 135.3 %all-to-all-start = ((bf16[128,16,1280]{2,1,0:T(8,128)(2,1)}), bf16[128,16,1280]{2,1,0:T(8,128)(2,1)}, u32[]{:S(2)}, u32[]{:S(2)}) async-start(bf16[128,16,1280]{2,1,0:T(8,128)(2,1)} %bitcast.32), calls=%async_computation | async-start | bytes 10485760 | tf_op jit(solution)/shard_map/all_to_all | solution.py:109
  35.2 166.2 %all-gather.6.cloned.1.call-start = ((), (), s32[]{:S(2)}) async-start(), calls=%async_computation.5 | async-start | bytes 1474560 | tf_op jit(solution)/shard_map/all_gather | solution.py:113
  167.5 175.2 %all-gather.8.cloned.1.call-start = ((), (), s32[]{:S(2)}) async-start(), calls=%async_computation.6 | async-start | bytes 6553600 | tf_op jit(solution)/shard_map/all_gather | solution.py:113
  201.5 163.9 %reduce-scatter.2.cloned.1.call-start = ((), (), s32[]{:S(2)}) async-start(), calls=%async_computation.4 | async-start | bytes 15728640 | tf_op jit(solution)/shard_map/reduce_scatter | solution.py:27
  365.4 14.4 %copy-start.7 = (s32[256]{0:T(256)S(1)}, s32[256]{0:T(256)}, u32[]{:S(2)}) copy-start(s32[256]{0:T(256)} %param.16) | copy-start | bytes 3076
  365.4 14.4 %copy-start.9 = (s32[128]{0:T(128)S(1)}, s32[128]{0:T(128)}, u32[]{:S(2)}) copy-start(s32[128]{0:T(128)} %param.15) | copy-start | bytes 1540
  365.4 14.6 %copy-start.8 = (s32[128]{0:T(128)S(1)}, s32[128]{0:T(128)}, u32[]{:S(2)}) copy-start(s32[128]{0:T(128)} %param.17) | copy-start | bytes 1540
  365.4 15.3 %copy-start.6 = (f32[128,6]{0,1:T(8,128)S(1)}, f32[128,6]{0,1:T(8,128)}, u32[]{:S(2)}) copy-start(f32[128,6]{0,1:T(8,128)} %param.14) | copy-start | bytes 9220
  365.4 134.7 %all-to-all-start.2 = ((bf16[128,16,1280]{2,1,0:T(8,128)(2,1)}), bf16[128,16,1280]{2,1,0:T(8,128)(2,1)}, u32[]{:S(2)}, u32[]{:S(2)}) async-start(bf16[128,16,1280]{2,1,0:T(8,128)(2,1)} %bitcast.34), calls=%async_computation.3 | async-start | bytes 10485760 | tf_op jit(solution)/shard_map/all_to_all | solution.py:126
  500.1 3.8 copy-start.1
  500.1 3.8 copy-start.3
Sparse Core Ops, SparseCore 0:
  167.6 33.7 all-gather.5
  203.2 57.5 all-gather.7
Sparse Core Ops, SparseCore 1:
  342.7 22.6 reduce-scatter.1
